TPU v7x, 128 devices: a whole 4x4x4 slice. The times are simulated.
128 devices in a mesh: shard: 32 (over x, y, core), tensor: 4 (over z).
Axes of the slice: x: 4, y: 4, z: 4, core: 2. Of those that a mesh axis runs over, the one named last changes fastest.
Arguments:
- grads: bfloat16 [384, 256, 256], P('shard', 'tensor'), may hold values from -60 to 60
- owner: int32 [384], replicated, may hold values from 0 to 31, as said below
- slot: int32 [384], replicated, may hold values from 0 to 23, as said below
- stat_left: float32 [768, 256, 256], P('shard', 'tensor'), may hold values from -144 to 2704, as said below
- stat_right: float32 [768, 256, 256], P('shard', 'tensor'), may hold values from -144 to 2704, as said below
- root_left: float32 [768, 256, 256], P('shard', 'tensor'), may hold values from -0.72 to 2.72, as said below
- root_right: float32 [768, 256, 256], P('shard'), may hold values from -0.72 to 2.72, as said below
- moment: float32 [768, 256, 256], P('shard', 'tensor'), may hold values from 0.1 to 10
- momentum: float32 [768, 256, 256], P('shard', 'tensor'), may hold values from -6 to 6
- master: float32 [768, 256, 256], P('shard', 'tensor'), may hold values from -0.3 to 0.3
Outputs:
- stat_left_new: float32 [768, 256, 256], P('shard', 'tensor')
- stat_right_new: float32 [768, 256, 256], P('shard', 'tensor')
- moment_new: float32 [768, 256, 256], P('shard', 'tensor')
- momentum_new: float32 [768, 256, 256], P('shard', 'tensor')
- master_new: float32 [768, 256, 256], P('shard', 'tensor')
- weights_new: bfloat16 [384, 256, 256], P('shard', 'tensor')
Inputs may be any that keep to these rules, and one draw needn't show every extreme that they name: Each owner group holds at most 24 blocks, some exactly 24; no owner group holds two blocks of one shard group (blocks b with equal b // 12). `slot`: the blocks of one owner group have distinct slots. `stat_left`: Symmetric. `stat_right`: Symmetric. `root_left`: Symmetric. `root_right`: Symmetric.
All inputs are finite; a program needn't handle non-finite values.
Results may differ from a plain program's by a relative error of at most 0.001.
Values may be sent and summed in bfloat16 or wider, within the bound.
No kernel may reach another device: no remote copies, remote signals or barrier semaphores. Data moves between devices by JAX's collectives and lax.ppermute only.
A program may use at most 128 MiB of HBM per device.

v0:
```python
import jax
import jax.numpy as jnp
from jax import lax
from jax.sharding import PartitionSpec as P

beta_stat = 0.95
beta_mom = 0.9
learn_rate = 0.01
eps_root = 1e-08
eps_mean = 1e-06


def on_device(
    grads, owner, slot, stat_left, stat_right, root_left, root_right, moment, momentum, master
):
    groups = lax.axis_size("shard")
    splits = lax.axis_size("tensor")
    slots_dev = stat_left.shape[0]
    rows_dev = stat_left.shape[1]
    order = stat_left.shape[2]
    blocks_group = grads.shape[0]
    shard_index = lax.axis_index("shard")
    tensor_index = lax.axis_index("tensor")
    owner_grid = owner.reshape(groups, blocks_group)
    slot_grid = slot.reshape(groups, blocks_group)
    local_owner = lax.dynamic_index_in_dim(owner_grid, shard_index, 0, keepdims=False)
    hit_mask = owner_grid == shard_index
    slot_ids = jnp.arange(slots_dev, dtype=jnp.int32)
    select = jnp.sum(
        (slot_grid[None, :, :] == slot_ids[:, None, None]) & hit_mask[None, :, :], axis=2
    ).astype(jnp.bfloat16)
    group_ids = jnp.arange(groups, dtype=jnp.int32)
    picker = (local_owner[None, :] == group_ids[:, None]).astype(jnp.bfloat16)
    row_start = tensor_index * rows_dev
    whole_rows = lax.all_gather(grads, "tensor", axis=1, tiled=True)
    outgoing = jnp.einsum(
        "gi,ixy->gxy", picker, whole_rows, preferred_element_type=jnp.float32
    ).astype(jnp.bfloat16)
    arrived = lax.all_to_all(outgoing, "shard", split_axis=0, concat_axis=0, tiled=True)
    grad_whole = jnp.einsum(
        "kg,gxy->kxy", select, arrived, preferred_element_type=jnp.float32
    ).astype(jnp.bfloat16)
    grad_piece = lax.dynamic_slice_in_dim(grad_whole, row_start, rows_dev, 1)
    highest = lax.Precision.HIGHEST
    grad_full = grad_whole.astype(jnp.float32)
    grad_rows = grad_piece.astype(jnp.float32)
    grad_cols = lax.dynamic_slice_in_dim(grad_full, row_start, rows_dev, 2)
    left_new = beta_stat * stat_left + (1.0 - beta_stat) * jnp.einsum(
        "kij,klj->kil", grad_rows, grad_full, precision=highest
    )
    right_new = beta_stat * stat_right + (1.0 - beta_stat) * jnp.einsum(
        "kji,kjl->kil", grad_cols, grad_full, precision=highest
    )
    second_new = beta_stat * moment + (1.0 - beta_stat) * grad_rows * grad_rows
    adam_step = grad_rows / (jnp.sqrt(second_new) + eps_root)
    precond = jnp.einsum("kij,kjl->kil", root_left, grad_full, precision=highest)
    precond = jnp.einsum("kij,kjl->kil", precond, root_right, precision=highest)
    adam_sum, precond_sum = lax.psum(
        (jnp.sum(adam_step * adam_step, axis=(1, 2)), jnp.sum(precond * precond, axis=(1, 2))),
        "tensor",
    )
    entries = float(rows_dev * splits * order)
    scale_ratio = jnp.sqrt(adam_sum / entries + eps_mean) / jnp.sqrt(
        precond_sum / entries + eps_mean
    )
    velocity_new = beta_mom * momentum + (1.0 - beta_mom) * scale_ratio[:, None, None] * precond
    weight_new = master - learn_rate * velocity_new
    weight_half = weight_new.astype(jnp.bfloat16)
    returning = jnp.einsum(
        "kg,kxy->gxy", select, weight_half, preferred_element_type=jnp.float32
    ).astype(jnp.bfloat16)
    back_rows = lax.all_to_all(returning, "shard", split_axis=0, concat_axis=0, tiled=True)
    weights_local = jnp.take(back_rows, local_owner, axis=0)
    return (left_new, right_new, second_new, velocity_new, weight_new, weights_local)


def solution(mesh):
    placed = (
        P("shard", "tensor", None),
        P(),
        P(),
        P("shard", "tensor", None),
        P("shard", "tensor", None),
        P("shard", "tensor", None),
        P("shard", None, None),
        P("shard", "tensor", None),
        P("shard", "tensor", None),
        P("shard", "tensor", None),
    )
    return jax.shard_map(
        on_device,
        mesh=mesh,
        in_specs=placed,
        out_specs=(
            P("shard", "tensor", None),
            P("shard", "tensor", None),
            P("shard", "tensor", None),
            P("shard", "tensor", None),
            P("shard", "tensor", None),
            P("shard", "tensor", None),
        ),
        check_vma=False,
    )
```

profile of v0, /device:TPU:1, one launch (start us, length us, event | category | flops | bytes accessed | tf_op | source)
XLA Modules:
  0.0 176.2 jit_solution(17148994907368642026)
XLA Ops:
  7.2 0.0 copy-start
  7.2 0.0 all-gather.2.cloned.1.call-start
  7.2 0.7 all-gather.2.cloned.1.call-update
  7.9 0.8 reshape.57
  8.7 30.7 %all-gather.2.cloned.1.call-done = bf16[12,256,256]{2,1,0:T(8,128)(2,1)} async-done(((bf16[12,64,256]{2,1,0:T(8,128)(2,1)}), bf16[12,256,256]{2,1,0:T(8,128)(2,1)}) %all-gather.2.cloned.1.call-update) | async-done | bytes 1572880 | tf_op jit(solution)/shard_map/all_gather | solution.py:35
  39.4 2.8 %convolution_convert_fusion = bf16[32,256,256]{2,0,1:T(8,128)(2,1)S(1)} fusion(bf16[12,256,256]{2,1,0:T(8,128)(2,1)} %all-gather.2.cloned.1.call-done, s32[12]{0:T(128)S(1)} %get-tuple-element.39), kind=kOutput, calls=%fused_computation.3 | convolution fusion | flops 52429184 | bytes 5767216 | tf_op jit(solution)/shard_map/gi,ixy->gxy/dot_general | solution.py:36
  42.2 4.4 %copy.84 = bf16[32,256,256]{2,1,0:T(8,128)(2,1)} copy(bf16[32,256,256]{2,0,1:T(8,128)(2,1)S(1)} %convolution_convert_fusion) | data formatting | bytes 8388608 | tf_op jit(solution)/shard_map/convert_element_type | solution.py:38
  46.6 0.0 copy-start.6
  46.6 8.1 %all-to-all-start = ((bf16[32,256,256]{2,1,0:T(8,128)(2,1)}), bf16[32,256,256]{2,1,0:T(8,128)(2,1)}, u32[]{:S(2)}, u32[]{:S(2)}) async-start(bf16[32,256,256]{2,1,0:T(8,128)(2,1)} %copy.84), calls=%async_computation | async-start | bytes 8388608 | tf_op jit(solution)/shard_map/all_to_all | solution.py:39
  54.7 0.1 copy.82
  54.8 0.0 copy-done.6
  54.8 0.1 eq.40
  54.9 0.1 copy.81
  55.0 51.6 %all-to-all-done = bf16[32,256,256]{2,1,0:T(8,128)(2,1)} async-done(((bf16[32,256,256]{2,1,0:T(8,128)(2,1)}), bf16[32,256,256]{2,1,0:T(8,128)(2,1)}, u32[]{:S(2)}, u32[]{:S(2)}) %all-to-all-start) | async-done | bytes 4194336 | tf_op jit(solution)/shard_map/all_to_all | solution.py:39
  106.6 4.7 %fusion.8 = bf16[24,256,256]{2,0,1:T(8,128)(2,1)S(1)} fusion(bf16[32,256,256]{2,1,0:T(8,128)(2,1)} %all-to-all-done, s32[24,32]{1,0:T(8,128)S(1)} %convert_reduce_fusion), kind=kOutput, calls=%fused_computation.11 | convolution fusion | flops 102236928 | bytes 7343104 | tf_op jit(solution)/shard_map/kg,gxy->kxy/dot_general | solution.py:40
  111.2 0.0 copy-start.1
  111.3 0.0 copy-start.3
  111.3 0.5 constant_dynamic-slice_fusion
  111.8 2.0 %copy-done.3 = f32[24,64,256]{2,1,0:T(8,128)S(1)} copy-done((f32[24,64,256]{2,1,0:T(8,128)S(1)}, f32[24,64,256]{2,1,0:T(8,128)}, u32[]{:S(2)}) %copy-start.3) | copy-done | bytes 1572888
  113.8 1.5 fusion.17
  115.3 0.0 copy-start.4
  115.3 0.8 fusion.4
  116.1 0.6 copy-done.4
  116.7 0.0 slice-start
  116.7 1.8 %fusion.14 = f32[24,64,256]{2,0,1:T(8,128)S(1)} fusion(f32[24,64,256]{2,1,0:T(8,128)S(1)} %fusion.4, f32[24,64,256]{2,1,0:T(8,128)S(1)} %copy-done.4), kind=kLoop, calls=%fused_computation.18 | loop fusion | flops 1179648 | bytes 4718592 | tf_op jit(solution)/shard_map/add | solution.py:51
  118.5 0.0 slice-start.1
  118.5 1.6 copy.98
  120.1 0.0 copy-done.1
  120.1 0.0 copy-done
  120.2 2.0 %fusion.2 = f32[24,256,64]{1,2,0:T(8,128)S(1)} fusion(f32[24,64,256]{2,1,0:T(8,128)S(1)} %copy-done, bf16[24,256,256]{2,0,1:T(8,128)(2,1)S(1)} %fusion.8), kind=kOutput, calls=%fused_computation.4 | convolution fusion | flops 1207959552 | bytes 6291456 | tf_op jit(solution)/shard_map/kij,kjl->kil/dot_general | solution.py:56
  122.1 0.0 slice-done
  122.1 0.0 slice-done.1
  122.2 5.3 %multiply_reduce_fusion = (f32[24]{0:T(128)S(1)}, f32[24,64,256]{2,1,0:T(8,128)}) fusion(f32[24,256,64]{1,2,0:T(8,128)S(1)} %fusion.2, f32[24,256,256]{2,1,0:T(8,128)S(1)} %bitcast.19), kind=kOutput, calls=%fused_computation.26 | convolution fusion | flops 1208745984 | bytes 9437280 | tf_op jit(solution)/shard_map/kij,kjl->kil/dot_general | solution.py:57
  127.5 7.4 %all-reduce = (f32[24]{0:T(128)S(1)}, f32[24]{0:T(128)S(1)}) all-reduce(f32[24]{0:T(128)S(1)} %get-tuple-element.45, f32[24]{0:T(128)S(1)} %get-tuple-element.43), channel_id=1, replica_groups=mesh['shard'=32,'tensor'=4] {'tensor'}, use_global_device_ids=true, to_apply=%region_4.5 | all-reduce | flops 48 | bytes 384 | tf_op jit(solution)/shard_map/psum | solution.py:58
  134.9 4.8 %fusion.31 = (bf16[24,64,256]{2,1,0:T(8,128)(2,1)S(1)}, f32[24,64,256]{2,1,0:T(8,128)}, f32[24,64,256]{2,1,0:T(8,128)}) fusion(f32[24,64,256]{2,1,0:T(8,128)} %param.19, f32[24,64,256]{2,1,0:T(8,128)} %get-tuple-element.46, f32[24]{0:T(128)S(1)} %multiply_multiply_fusion.1, f32[24,64,256]{2,1,0:T(8,128)} %param.18), kind=kLoop, calls=%fused_computation.53 | loop fusion | flops 2359296 | bytes 8650848 | tf_op jit(solution)/shard_map/convert_element_type | solution.py:68
  139.7 0.7 convolution_convert_fusion.1
  140.4 1.6 copy.96
  142.0 9.1 %all-to-all-start.1 = ((bf16[32,64,256]{2,1,0:T(8,128)(2,1)}), bf16[32,64,256]{2,1,0:T(8,128)(2,1)S(1)}, u32[]{:S(2)}, u32[]{:S(2)}) async-start(bf16[32,64,256]{2,1,0:T(8,128)(2,1)} %copy.96), calls=%async_computation.1 | async-start | bytes 2097152 | tf_op jit(solution)/shard_map/all_to_all | solution.py:72
  151.1 2.5 %fusion.13 = f32[24,64,256]{2,0,1:T(8,128)S(1)} fusion(bf16[24,64,256]{2,0,1:T(8,128)(2,1)S(1)} %get-tuple-element.44, f32[24,64,256]{2,1,0:T(8,128)} %param.17), kind=kLoop, calls=%fused_computation.15 | loop fusion | flops 1966080 | bytes 3932160 | tf_op jit(solution)/shard_map/add | solution.py:54
  153.5 1.6 copy.99
  155.2 0.8 copy-done.2
  156.0 1.1 fusion.6
  157.1 0.3 copy-done.5
  157.4 1.8 %fusion.16 = f32[24,64,256]{2,0,1:T(8,128)S(1)} fusion(f32[24,64,256]{2,1,0:T(8,128)S(1)} %fusion.6, f32[24,64,256]{2,1,0:T(8,128)S(1)} %copy-done.5), kind=kLoop, calls=%fused_computation.22 | loop fusion | flops 1179648 | bytes 4718592 | tf_op jit(solution)/shard_map/add | solution.py:48
  159.2 1.6 copy.97
  160.9 7.1 %all-to-all-done.1 = bf16[32,64,256]{2,1,0:T(8,128)(2,1)S(1)} async-done(((bf16[32,64,256]{2,1,0:T(8,128)(2,1)}), bf16[32,64,256]{2,1,0:T(8,128)(2,1)S(1)}, u32[]{:S(2)}, u32[]{:S(2)}) %all-to-all-start.1) | async-done | bytes 1048608 | tf_op jit(solution)/shard_map/all_to_all | solution.py:72
  168.0 0.6 gather_fusion
  168.5 0.9 broadcast_select_fusion
  (9 shorter events, 0.1 us)
Async XLA Ops:
  7.2 113.0 %copy-start = (f32[24,64,256]{2,1,0:T(8,128)S(1)}, f32[24,64,256]{2,1,0:T(8,128)}, u32[]{:S(2)}) copy-start(f32[24,64,256]{2,1,0:T(8,128)} %param.15) | copy-start | bytes 4718596
  7.2 32.2 %all-gather.2.cloned.1.call-start = ((), (), s32[]{:S(2)}) async-start(), calls=%async_computation.2 | async-start | bytes 1966080 | tf_op jit(solution)/shard_map/all_gather | solution.py:35
  46.6 8.2 %copy-start.6 = (s32[384]{0:T(512)S(1)}, s32[384]{0:T(512)}, u32[]{:S(2)}) copy-start(s32[384]{0:T(512)} %param.12) | copy-start | bytes 4612
  46.6 60.0 %all-to-all-start = ((bf16[32,256,256]{2,1,0:T(8,128)(2,1)}), bf16[32,256,256]{2,1,0:T(8,128)(2,1)}, u32[]{:S(2)}, u32[]{:S(2)}) async-start(bf16[32,256,256]{2,1,0:T(8,128)(2,1)} %copy.84), calls=%async_computation | async-start | bytes 8388608 | tf_op jit(solution)/shard_map/all_to_all | solution.py:39
  111.2 8.9 %copy-start.1 = (bf16[24,256,256]{2,0,1:T(8,128)(2,1)}, bf16[24,256,256]{2,0,1:T(8,128)(2,1)S(1)}, u32[]{:S(2)}) copy-start(bf16[24,256,256]{2,0,1:T(8,128)(2,1)S(1)} %fusion.8) | copy-start | bytes 9437188
  111.3 2.5 %copy-start.3 = (f32[24,64,256]{2,1,0:T(8,128)S(1)}, f32[24,64,256]{2,1,0:T(8,128)}, u32[]{:S(2)}) copy-start(f32[24,64,256]{2,1,0:T(8,128)} %param.17) | copy-start | bytes 4718596
  115.3 1.4 copy-start.4
  116.7 5.5 %slice-start = ((s8[6291456]{0:T(1024)(128)(4,1)}), s8[4194304]{0:T(1024)(128)(4,1)S(1)}, s32[]{:S(2)}) async-start(s8[6291456]{0:T(1024)(128)(4,1)} %bitcast.18), calls=%async_computation.3 | async-start | bytes 8388608
  118.5 3.6 %slice-start.1 = ((s8[6291456]{0:T(1024)(128)(4,1)}), s8[2097152]{0:T(1024)(128)(4,1)S(1)}, s32[]{:S(2)}) async-start(s8[6291456]{0:T(1024)(128)(4,1)} %bitcast.18), calls=%async_computation.4 | async-start | bytes 4194304
  142.0 26.0 %all-to-all-start.1 = ((bf16[32,64,256]{2,1,0:T(8,128)(2,1)}), bf16[32,64,256]{2,1,0:T(8,128)(2,1)S(1)}, u32[]{:S(2)}, u32[]{:S(2)}) async-start(bf16[32,64,256]{2,1,0:T(8,128)(2,1)} %copy.96), calls=%async_computation.1 | async-start | bytes 2097152 | tf_op jit(solution)/shard_map/all_to_all | solution.py:72
  153.5 2.5 %copy-start.2 = (bf16[24,256,256]{2,0,1:T(8,128)(2,1)S(1)}, bf16[24,256,256]{2,0,1:T(8,128)(2,1)}, u32[]{:S(2)}) copy-start(bf16[24,256,256]{2,0,1:T(8,128)(2,1)} %copy-done.1) | copy-start | bytes 9437188
  156.0 1.4 copy-start.5
Sparse Core Ops, SparseCore 0:
  9.7 29.6 all-gather.1
where the time goes:
time: 177 us; the launch traced here: 176 us
  waiting for transfers between devices  90 us (51%)
  matrix products  17.3 us (10%)
  starting transfers between devices  17.2 us (10%)
  local copies, waits for them, and re-layouts  16.8 us (9%)
  between operations  14.2 us (8%)
  other arithmetic  13.4 us (8%)
  blocking collectives  7.38 us (4%)
    all_to_all x1, waiting for transfers between devices, on_device(): lax.all_to_all(outgoing, 'shard', split_axis=0, concat_axis=0, tiled=True)  51.6 us
    all_gather x1, waiting for transfers between devices, on_device(): whole_rows = lax.all_gather(grads, 'tensor', axis=1, tiled=True)  30.7 us
    all_to_all x1, starting transfers between devices, on_device(): lax.all_to_all(returning, 'shard', split_axis=0, concat_axis=0, tiled=True)  9.05 us
    unnamed x21, local copies, waits for them, and re-layouts  8.7 us
    all_to_all x1, starting transfers between devices, on_device(): lax.all_to_all(outgoing, 'shard', split_axis=0, concat_axis=0, tiled=True)  8.06 us
    psum x1, blocking collectives, on_device(): lax.psum((jnp.sum(adam_step * adam_step, axis=(1, 2)), jnp.sum(precond *...  7.38 us
    all_to_all x1, waiting for transfers between devices, on_device(): lax.all_to_all(returning, 'shard', split_axis=0, concat_axis=0, tiled=True)  7.11 us
    dot_general x1, matrix products, on_device(): precond = jnp.einsum('kij,kjl->kil', precond, root_right, precision=highest)  5.35 us
  transfers between devices with their start and end apart: 3, of which 3 were waited for; matrix products, arithmetic and copies ran while one was open for 6% of the time, Pallas kernels for 0%

commit v1 on v0

--- a/solution.py
+++ b/solution.py
@@ -8,6 +8,22 @@
 learn_rate = 0.01
 eps_root = 1e-08
 eps_mean = 1e-06
+
+
+def gather_around(x, axis, dim):
+    ways, here, turn = (lax.axis_size(axis), lax.axis_index(axis), x.shape[dim])
+    lengths = [n * ways if d == dim else n for d, n in enumerate(x.shape)]
+    full = lax.dynamic_update_slice_in_dim(jnp.zeros(lengths, x.dtype), x, here * turn, axis=dim)
+    going_up = going_down = x
+    for far in range(1, ways // 2 + 1):
+        going_up = lax.ppermute(going_up, axis, [(d, (d + 1) % ways) for d in range(ways)])
+        full = lax.dynamic_update_slice_in_dim(full, going_up, (here - far) % ways * turn, axis=dim)
+        if 2 * far < ways:
+            going_down = lax.ppermute(going_down, axis, [(d, (d - 1) % ways) for d in range(ways)])
+            full = lax.dynamic_update_slice_in_dim(
+                full, going_down, (here + far) % ways * turn, axis=dim
+            )
+    return full
 
 
 def on_device(
@@ -32,7 +48,7 @@
     group_ids = jnp.arange(groups, dtype=jnp.int32)
     picker = (local_owner[None, :] == group_ids[:, None]).astype(jnp.bfloat16)
     row_start = tensor_index * rows_dev
-    whole_rows = lax.all_gather(grads, "tensor", axis=1, tiled=True)
+    whole_rows = gather_around(grads, "tensor", 1)
     outgoing = jnp.einsum(
         "gi,ixy->gxy", picker, whole_rows, preferred_element_type=jnp.float32
     ).astype(jnp.bfloat16)

time: 177 us -> 157 us (0.89)
  waiting for transfers between devices: 90 us -> 73.6 us
  between operations: 14.2 us -> 0.84 us
  starting transfers between devices: 17.2 us -> 23.3 us
  local copies, waits for them, and re-layouts: 16.8 us -> 21.7 us
    all_gather x1 -> x0, waiting for transfers between devices: 30.7 us -> none  [on_device(): whole_rows = lax.all_gather(grads, 'tensor', axis=1, tiled=True)]
    ppermute x0 -> x3, waiting for transfers between devices: none -> 14.9 us  [the longest x2 14.9 us: gather_around(): lax.ppermute(going_up, axis, [(d, (d + 1) % ways) for d in range(ways)])]
    ppermute x0 -> x3, starting transfers between devices: none -> 4.73 us  [the longest x2 2.53 us: gather_around(): lax.ppermute(going_up, axis, [(d, (d + 1) % ways) for d in range(ways)])]
    dynamic_update_slice x0 -> x4, local copies, waits for them, and re-layouts: none -> 4.11 us  [the longest x2 2.08 us: gather_around(): lax.dynamic_update_slice_in_dim(full, going_up, (here - far) % ways * tur...]
    unnamed x21 -> x25, local copies, waits for them, and re-layouts: 8.7 us -> 8.71 us
  transfers between devices with their start and end apart: 3 -> 5, of which waited for: 3 -> 4; matrix products, arithmetic and copies ran while one was open for 6% -> 9% of each run, Pallas kernels for 0% -> 0%
where the time goes in v1:
time: 157 us; the launch traced here: 156 us
  waiting for transfers between devices  73.6 us (47%)
  starting transfers between devices  23.3 us (15%)
  local copies, waits for them, and re-layouts  21.7 us (14%)
  matrix products  17.5 us (11%)
  other arithmetic  13.4 us (9%)
  blocking collectives  5.97 us (4%)
    all_to_all x1, waiting for transfers between devices, on_device(): lax.all_to_all(outgoing, 'shard', split_axis=0, concat_axis=0, tiled=True)  51.6 us
    ppermute x2, waiting for transfers between devices, gather_around(): lax.ppermute(going_up, axis, [(d, (d + 1) % ways) for d in range(ways)])  14.9 us
    all_to_all x1, starting transfers between devices, on_device(): lax.all_to_all(outgoing, 'shard', split_axis=0, concat_axis=0, tiled=True)  9.55 us
    all_to_all x1, starting transfers between devices, on_device(): lax.all_to_all(returning, 'shard', split_axis=0, concat_axis=0, tiled=True)  8.97 us
    unnamed x25, local copies, waits for them, and re-layouts  8.71 us
    all_to_all x1, waiting for transfers between devices, on_device(): lax.all_to_all(returning, 'shard', split_axis=0, concat_axis=0, tiled=True)  7.11 us
    psum x1, blocking collectives, on_device(): lax.psum((jnp.sum(adam_step * adam_step, axis=(1, 2)), jnp.sum(precond *...  5.97 us
    dot_general x1, matrix products, on_device(): precond = jnp.einsum('kij,kjl->kil', precond, root_right, precision=highest)  5.35 us
  transfers between devices with their start and end apart: 5, of which 4 were waited for; matrix products, arithmetic and copies ran while one was open for 9% of the time, Pallas kernels for 0%

profile of v1, /device:TPU:1, one launch (start us, length us, event | category | flops | bytes accessed | tf_op | source)
XLA Modules:
  0.0 156.2 jit_solution(18041398864201228234)
XLA Ops:
  0.6 0.0 copy-start
  0.7 2.5 %collective-permute-start = (bf16[12,64,256]{2,1,0:T(8,128)(2,1)}, bf16[12,64,256]{2,1,0:T(8,128)(2,1)S(1)}, u32[]{:S(2)}, u32[]{:S(2)}) collective-permute-start(bf16[12,64,256]{2,1,0:T(8,128)(2,1)} %param.10), channel_id=1, source_target_pairs={{0,1},{1,2},{2,3},{3,0},{4,5},{5,6},{6,7},{7,4},{8,9},{9,10},{10,1... | collective-permute-start | bytes 1179656 | tf_op jit(solution)/shard_map/ppermute | solution.py:19
  3.2 2.2 %collective-permute-start.1 = (bf16[12,64,256]{2,1,0:T(8,128)(2,1)}, bf16[12,64,256]{2,1,0:T(8,128)(2,1)S(1)}, u32[]{:S(2)}, u32[]{:S(2)}) collective-permute-start(bf16[12,64,256]{2,1,0:T(8,128)(2,1)} %param.10), channel_id=1, source_target_pairs={{0,3},{1,0},{2,1},{3,2},{4,7},{5,4},{6,5},{7,6},{8,11},{9,8},{10,9... | collective-permute-start | bytes 1179656 | tf_op jit(solution)/shard_map/ppermute | solution.py:22
  5.4 1.5 broadcast_in_dim.18
  6.9 1.0 copy_dynamic-update-slice_fusion.3
  7.9 0.1 reshape.57
  8.0 6.3 %collective-permute-done = bf16[12,64,256]{2,1,0:T(8,128)(2,1)S(1)} collective-permute-done((bf16[12,64,256]{2,1,0:T(8,128)(2,1)}, bf16[12,64,256]{2,1,0:T(8,128)(2,1)S(1)}, u32[]{:S(2)}, u32[]{:S(2)}) %collective-permute-start) | collective-permute-done | bytes 393248 | tf_op jit(solution)/shard_map/ppermute | solution.py:19
  14.3 0.0 collective-permute-start.2
  14.3 1.0 copy_dynamic-update-slice_fusion.2
  15.4 0.0 collective-permute-done.1
  15.4 1.0 copy_dynamic-update-slice_fusion.1
  16.4 8.6 %collective-permute-done.2 = bf16[12,64,256]{2,1,0:T(8,128)(2,1)S(1)} collective-permute-done((bf16[12,64,256]{2,1,0:T(8,128)(2,1)S(1)}, bf16[12,64,256]{2,1,0:T(8,128)(2,1)S(1)}, u32[]{:S(2)}, u32[]{:S(2)}) %collective-permute-start.2) | collective-permute-done | bytes 393248 | tf_op jit(solution)/shard_map/ppermute | solution.py:19
  25.0 1.1 copy_dynamic-update-slice_fusion
  26.0 2.9 %convolution_convert_fusion = bf16[32,256,256]{2,0,1:T(8,128)(2,1)S(1)} fusion(bf16[12,256,256]{2,0,1:T(8,128)(2,1)} %copy_dynamic-update-slice_fusion, s32[12]{0:T(128)S(1)} %get-tuple-element.33), kind=kOutput, calls=%fused_computation.3 | convolution fusion | flops 52429184 | bytes 5767216 | tf_op jit(solution)/shard_map/gi,ixy->gxy/dot_general | solution.py:52
  29.0 4.4 %copy.72 = bf16[32,256,256]{2,1,0:T(8,128)(2,1)} copy(bf16[32,256,256]{2,0,1:T(8,128)(2,1)S(1)} %convolution_convert_fusion) | data formatting | bytes 8388608 | tf_op jit(solution)/shard_map/convert_element_type | solution.py:54
  33.4 9.6 %all-to-all-start = ((bf16[32,256,256]{2,1,0:T(8,128)(2,1)}), bf16[32,256,256]{2,1,0:T(8,128)(2,1)}, u32[]{:S(2)}, u32[]{:S(2)}) async-start(bf16[32,256,256]{2,1,0:T(8,128)(2,1)} %copy.72), calls=%async_computation | async-start | bytes 8388608 | tf_op jit(solution)/shard_map/all_to_all | solution.py:55
  42.9 0.1 copy.67
  43.0 0.1 eq.44
  43.2 0.1 copy.66
  43.3 51.6 %all-to-all-done = bf16[32,256,256]{2,1,0:T(8,128)(2,1)} async-done(((bf16[32,256,256]{2,1,0:T(8,128)(2,1)}), bf16[32,256,256]{2,1,0:T(8,128)(2,1)}, u32[]{:S(2)}, u32[]{:S(2)}) %all-to-all-start) | async-done | bytes 4194336 | tf_op jit(solution)/shard_map/all_to_all | solution.py:55
  94.9 4.7 %fusion.8 = bf16[24,256,256]{2,0,1:T(8,128)(2,1)S(1)} fusion(bf16[32,256,256]{2,1,0:T(8,128)(2,1)} %all-to-all-done, s32[24,32]{1,0:T(8,128)S(1)} %convert_reduce_fusion), kind=kOutput, calls=%fused_computation.11 | convolution fusion | flops 102236928 | bytes 7343104 | tf_op jit(solution)/shard_map/kg,gxy->kxy/dot_general | solution.py:56
  99.5 0.0 copy-start.3
  99.6 0.5 constant_dynamic-slice_fusion
  100.1 2.0 %copy-done.3 = f32[24,64,256]{2,1,0:T(8,128)S(1)} copy-done((f32[24,64,256]{2,1,0:T(8,128)S(1)}, f32[24,64,256]{2,1,0:T(8,128)}, u32[]{:S(2)}) %copy-start.3) | copy-done | bytes 1572888
  102.1 1.5 fusion.16
  103.6 0.8 fusion.4
  104.4 0.6 copy-done.4
  105.0 1.8 %fusion.13 = f32[24,64,256]{2,0,1:T(8,128)S(1)} fusion(f32[24,64,256]{2,1,0:T(8,128)S(1)} %fusion.4, f32[24,64,256]{2,1,0:T(8,128)S(1)} %copy-done.4), kind=kLoop, calls=%fused_computation.17 | loop fusion | flops 1179648 | bytes 4718592 | tf_op jit(solution)/shard_map/add | solution.py:67
  106.8 0.0 slice-start.1
  106.8 1.6 %copy.86 = f32[24,64,256]{2,1,0:T(8,128)} copy(f32[24,64,256]{2,0,1:T(8,128)S(1)} %fusion.13) | data formatting | bytes 3145728
  108.4 0.0 copy-done.1
  108.4 2.0 %fusion.2 = f32[24,256,64]{1,2,0:T(8,128)S(1)} fusion(f32[24,64,256]{2,1,0:T(8,128)S(1)} %copy-done, bf16[24,256,256]{2,0,1:T(8,128)(2,1)S(1)} %fusion.8), kind=kOutput, calls=%fused_computation.4 | convolution fusion | flops 1207959552 | bytes 6291456 | tf_op jit(solution)/shard_map/kij,kjl->kil/dot_general | solution.py:72
  110.4 5.3 %multiply_reduce_fusion = (f32[24]{0:T(128)S(1)}, f32[24,64,256]{2,1,0:T(8,128)}) fusion(f32[24,256,64]{1,2,0:T(8,128)S(1)} %fusion.2, f32[24,256,256]{2,1,0:T(8,128)S(1)} %bitcast.20), kind=kOutput, calls=%fused_computation.25 | convolution fusion | flops 1208745984 | bytes 9437280 | tf_op jit(solution)/shard_map/kij,kjl->kil/dot_general | solution.py:73
  115.8 6.0 %all-reduce = (f32[24]{0:T(128)S(1)}, f32[24]{0:T(128)S(1)}) all-reduce(f32[24]{0:T(128)S(1)} %get-tuple-element.39, f32[24]{0:T(128)S(1)} %get-tuple-element.37), channel_id=1, replica_groups=mesh['shard'=32,'tensor'=4] {'tensor'}, use_global_device_ids=true, to_apply=%region_4.5 | all-reduce | flops 48 | bytes 384 | tf_op jit(solution)/shard_map/psum | solution.py:74
  121.8 4.8 %fusion.30 = (bf16[24,64,256]{2,1,0:T(8,128)(2,1)S(1)}, f32[24,64,256]{2,1,0:T(8,128)}, f32[24,64,256]{2,1,0:T(8,128)}) fusion(f32[24,64,256]{2,1,0:T(8,128)} %param.19, f32[24,64,256]{2,1,0:T(8,128)} %get-tuple-element.40, f32[24]{0:T(128)S(1)} %multiply_multiply_fusion.1, f32[24,64,256]{2,1,0:T(8,128)} %param.18), kind=kLoop, calls=%fused_computation.56 | loop fusion | flops 2359296 | bytes 8650848 | tf_op jit(solution)/shard_map/convert_element_type | solution.py:84
  126.6 0.7 convolution_convert_fusion.1
  127.3 1.6 %copy.84 = bf16[32,64,256]{2,1,0:T(8,128)(2,1)} copy(bf16[32,64,256]{2,0,1:T(8,128)(2,1)S(1)} %convolution_convert_fusion.1) | data formatting | bytes 2097152 | tf_op jit(solution)/shard_map/convert_element_type | solution.py:87
  128.9 9.0 %all-to-all-start.1 = ((bf16[32,64,256]{2,1,0:T(8,128)(2,1)}), bf16[32,64,256]{2,1,0:T(8,128)(2,1)S(1)}, u32[]{:S(2)}, u32[]{:S(2)}) async-start(bf16[32,64,256]{2,1,0:T(8,128)(2,1)} %copy.84), calls=%async_computation.1 | async-start | bytes 2097152 | tf_op jit(solution)/shard_map/all_to_all | solution.py:88
  137.9 2.5 %fusion.12 = f32[24,64,256]{2,0,1:T(8,128)S(1)} fusion(bf16[24,64,256]{2,0,1:T(8,128)(2,1)S(1)} %get-tuple-element.38, f32[24,64,256]{2,1,0:T(8,128)} %param.17), kind=kLoop, calls=%fused_computation.14 | loop fusion | flops 1966080 | bytes 3932160 | tf_op jit(solution)/shard_map/add | solution.py:70
  140.3 1.6 %copy.87 = f32[24,64,256]{2,1,0:T(8,128)} copy(f32[24,64,256]{2,0,1:T(8,128)S(1)} %fusion.12) | data formatting | bytes 3145728
  142.0 0.8 copy-done.2
  142.8 1.1 fusion.6
  143.9 0.3 copy-done.5
  144.2 1.8 %fusion.15 = f32[24,64,256]{2,0,1:T(8,128)S(1)} fusion(f32[24,64,256]{2,1,0:T(8,128)S(1)} %fusion.6, f32[24,64,256]{2,1,0:T(8,128)S(1)} %copy-done.5), kind=kLoop, calls=%fused_computation.21 | loop fusion | flops 1179648 | bytes 4718592 | tf_op jit(solution)/shard_map/add | solution.py:64
  146.0 1.6 %copy.85 = f32[24,64,256]{2,1,0:T(8,128)} copy(f32[24,64,256]{2,0,1:T(8,128)S(1)} %fusion.15) | data formatting | bytes 3145728
  147.7 7.1 %all-to-all-done.1 = bf16[32,64,256]{2,1,0:T(8,128)(2,1)S(1)} async-done(((bf16[32,64,256]{2,1,0:T(8,128)(2,1)}), bf16[32,64,256]{2,1,0:T(8,128)(2,1)S(1)}, u32[]{:S(2)}, u32[]{:S(2)}) %all-to-all-start.1) | async-done | bytes 1048608 | tf_op jit(solution)/shard_map/all_to_all | solution.py:88
  154.8 0.6 gather_fusion
  155.3 0.9 broadcast_select_fusion
  (21 shorter events, 0.1 us)
Async XLA Ops:
  0.6 107.8 %copy-start = (f32[24,64,256]{2,1,0:T(8,128)S(1)}, f32[24,64,256]{2,1,0:T(8,128)}, u32[]{:S(2)}) copy-start(f32[24,64,256]{2,1,0:T(8,128)} %param.15) | copy-start | bytes 4718596
  0.6 6.2 %copy-start.6 = (bf16[12,64,256]{2,1,0:T(8,128)(2,1)S(1)}, bf16[12,64,256]{2,1,0:T(8,128)(2,1)}, u32[]{:S(2)}) copy-start(bf16[12,64,256]{2,1,0:T(8,128)(2,1)} %param.10) | copy-start | bytes 1179652
  0.7 7.2 %copy-start.7 = (s32[384]{0:T(512)S(1)}, s32[384]{0:T(512)}, u32[]{:S(2)}) copy-start(s32[384]{0:T(512)} %param.11) | copy-start | bytes 4612
  0.7 13.7 %collective-permute-start = (bf16[12,64,256]{2,1,0:T(8,128)(2,1)}, bf16[12,64,256]{2,1,0:T(8,128)(2,1)S(1)}, u32[]{:S(2)}, u32[]{:S(2)}) collective-permute-start(bf16[12,64,256]{2,1,0:T(8,128)(2,1)} %param.10), channel_id=1, source_target_pairs={{0,1},{1,2},{2,3},{3,0},{4,5},{5,6},{6,7},{7,4},{8,9},{9,10},{10,1... | collective-permute-start | bytes 1179656 | tf_op jit(solution)/shard_map/ppermute | solution.py:19
  3.2 12.2 %collective-permute-start.1 = (bf16[12,64,256]{2,1,0:T(8,128)(2,1)}, bf16[12,64,256]{2,1,0:T(8,128)(2,1)S(1)}, u32[]{:S(2)}, u32[]{:S(2)}) collective-permute-start(bf16[12,64,256]{2,1,0:T(8,128)(2,1)} %param.10), channel_id=1, source_target_pairs={{0,3},{1,0},{2,1},{3,2},{4,7},{5,4},{6,5},{7,6},{8,11},{9,8},{10,9... | collective-permute-start | bytes 1179656 | tf_op jit(solution)/shard_map/ppermute | solution.py:22
  14.3 10.6 %collective-permute-start.2 = (bf16[12,64,256]{2,1,0:T(8,128)(2,1)S(1)}, bf16[12,64,256]{2,1,0:T(8,128)(2,1)S(1)}, u32[]{:S(2)}, u32[]{:S(2)}) collective-permute-start(bf16[12,64,256]{2,1,0:T(8,128)(2,1)S(1)} %collective-permute-done), channel_id=1, source_target_pairs={{0,1},{1,2},{2,3},{3,0},{4,5},{5,6},{6,7},{7,4},{8,9},{9,10},{10,1... | collective-permute-start | bytes 1179656 | tf_op jit(solution)/shard_map/ppermute | solution.py:19
  33.4 9.7 %copy-start.8 = (s32[384]{0:T(512)S(1)}, s32[384]{0:T(512)}, u32[]{:S(2)}) copy-start(s32[384]{0:T(512)} %param.12) | copy-start | bytes 4612
  33.4 61.5 %all-to-all-start = ((bf16[32,256,256]{2,1,0:T(8,128)(2,1)}), bf16[32,256,256]{2,1,0:T(8,128)(2,1)}, u32[]{:S(2)}, u32[]{:S(2)}) async-start(bf16[32,256,256]{2,1,0:T(8,128)(2,1)} %copy.72), calls=%async_computation | async-start | bytes 8388608 | tf_op jit(solution)/shard_map/all_to_all | solution.py:55
  99.5 8.9 %copy-start.1 = (bf16[24,256,256]{2,0,1:T(8,128)(2,1)}, bf16[24,256,256]{2,0,1:T(8,128)(2,1)S(1)}, u32[]{:S(2)}) copy-start(bf16[24,256,256]{2,0,1:T(8,128)(2,1)S(1)} %fusion.8) | copy-start | bytes 9437188
  99.5 2.5 %copy-start.3 = (f32[24,64,256]{2,1,0:T(8,128)S(1)}, f32[24,64,256]{2,1,0:T(8,128)}, u32[]{:S(2)}) copy-start(f32[24,64,256]{2,1,0:T(8,128)} %param.17) | copy-start | bytes 4718596
  103.6 1.4 copy-start.4
  105.0 5.5 %slice-start = ((s8[6291456]{0:T(1024)(128)(4,1)}), s8[4194304]{0:T(1024)(128)(4,1)S(1)}, s32[]{:S(2)}) async-start(s8[6291456]{0:T(1024)(128)(4,1)} %bitcast.19), calls=%async_computation.2 | async-start | bytes 8388608
  106.8 3.6 %slice-start.1 = ((s8[6291456]{0:T(1024)(128)(4,1)}), s8[2097152]{0:T(1024)(128)(4,1)S(1)}, s32[]{:S(2)}) async-start(s8[6291456]{0:T(1024)(128)(4,1)} %bitcast.19), calls=%async_computation.3 | async-start | bytes 4194304
  128.9 25.9 %all-to-all-start.1 = ((bf16[32,64,256]{2,1,0:T(8,128)(2,1)}), bf16[32,64,256]{2,1,0:T(8,128)(2,1)S(1)}, u32[]{:S(2)}, u32[]{:S(2)}) async-start(bf16[32,64,256]{2,1,0:T(8,128)(2,1)} %copy.84), calls=%async_computation.1 | async-start | bytes 2097152 | tf_op jit(solution)/shard_map/all_to_all | solution.py:88
  140.3 2.5 %copy-start.2 = (bf16[24,256,256]{2,0,1:T(8,128)(2,1)S(1)}, bf16[24,256,256]{2,0,1:T(8,128)(2,1)}, u32[]{:S(2)}) copy-start(bf16[24,256,256]{2,0,1:T(8,128)(2,1)} %copy-done.1) | copy-start | bytes 9437188
  142.8 1.4 copy-start.5
